TPU v7x, 256 devices: a whole 4x4x8 slice. The times are simulated.
256 devices in a mesh: row: 8 (over z), col: 32 (over y, x, core).
Axes of the slice: x: 4, y: 4, z: 8, core: 2. Of those that a mesh axis runs over, the one named last changes fastest.
Arguments:
- hidden_in: bfloat16 [3072, 2, 7168], P('row', None, 'col'), may hold values from -16 to 16
- final_gain: float32 [2, 7168], P(None, 'col'), may hold values from 0.25 to 1.75
- unembed: bfloat16 [7168, 32768], P('row', 'col'), may hold values from -2 to 2
- lengths: int32 [16], replicated, may hold values from 1 to 768, 3072 in all
- targets: int32 [3072], P('row'), may hold values from 0 to 32767
- owner: int32 [16], replicated, may hold values from 0 to 31
Outputs:
- owner_table: float32 [32, 3, 16], P('col')
Inputs may be any that keep to these rules, and one draw needn't show every extreme that they name: The lengths sum to 3072; the longest is exactly 768.
All inputs are finite; a program needn't handle non-finite values.
Results may differ from a plain program's by a relative error of at most 0.00056.
Values may be sent and summed in bfloat16 or wider, within the bound.
No kernel may reach another device: no remote copies, remote signals or barrier semaphores. Data moves between devices by JAX's collectives and lax.ppermute only.
A program may use at most 128 MiB of HBM per device.

v0:
```python
import jax
import jax.numpy as jnp
from jax import lax
from jax.sharding import PartitionSpec as P

D = 7168
EPS = 1e-05


def per_device(hidden_in, final_gain, unembed, lengths, targets, owner):
    tok_rows = hidden_in.shape[0]
    vocab_cols = unembed.shape[1]
    col_index = lax.axis_index("col")
    row_index = lax.axis_index("row")
    full_unembed = lax.all_gather(unembed, "row", axis=0, tiled=True)
    full_hidden = lax.all_gather(hidden_in, "col", axis=2, tiled=True)
    full_gain = lax.all_gather(final_gain, "col", axis=1, tiled=True)
    stream = full_hidden.astype(jnp.float32)
    mean_square = jnp.sum(stream * stream, axis=2) / D
    features = (stream * lax.rsqrt(mean_square[:, :, None] + EPS) * full_gain[None, :, :]).astype(
        jnp.bfloat16
    )
    logits = jnp.einsum("tmd,dv->tmv", features, full_unembed, preferred_element_type=jnp.float32)
    row_max = jnp.max(logits, axis=2)
    exp_total = jnp.sum(jnp.exp(logits - row_max[:, :, None]), axis=2)
    vocab_ids = col_index * vocab_cols + jnp.arange(vocab_cols, dtype=jnp.int32)
    picked = jnp.sum(
        jnp.where(targets[:, None, None] == vocab_ids[None, None, :], logits, 0.0), axis=2
    )
    parts = lax.all_gather(jnp.stack([row_max, exp_total, picked]), "col")
    max_logit = jnp.max(parts[:, 0], axis=0)
    exp_total = jnp.sum(parts[:, 1] * jnp.exp(parts[:, 0] - max_logit[None]), axis=0)
    picked = jnp.sum(parts[:, 2], axis=0)
    logp = picked - (max_logit + jnp.log(exp_total))
    log_ratio = logp[:, 0] - logp[:, 1]
    token_index = row_index * tok_rows + jnp.arange(tok_rows, dtype=jnp.int32)
    seq_ends = jnp.cumsum(lengths)
    segment = jnp.sum((seq_ends[None, :] <= token_index[:, None]).astype(jnp.int32), axis=1)
    member = segment[:, None] == jnp.arange(lengths.shape[0], dtype=jnp.int32)[None, :]
    ratio_sums = jnp.sum(jnp.where(member, log_ratio[:, None], 0.0), axis=0)
    squares = jnp.sum(jnp.where(member, (log_ratio * log_ratio)[:, None], 0.0), axis=0)
    ratio_max = jnp.max(jnp.where(member, log_ratio[:, None], -1e30), axis=0)
    stats = lax.all_gather(jnp.stack([ratio_sums, squares, ratio_max]), "row")
    seq_stats = jnp.stack(
        [jnp.sum(stats[:, 0], axis=0), jnp.sum(stats[:, 1], axis=0), jnp.max(stats[:, 2], axis=0)]
    )
    owned = owner == col_index
    return jnp.where(owned[None, :], seq_stats, 0.0)[None]


def solution(mesh):
    in_specs = (P("row", None, "col"), P(None, "col"), P("row", "col"), P(), P("row"), P())
    out_specs = P("col", None, None)
    return jax.shard_map(
        per_device, mesh=mesh, in_specs=in_specs, out_specs=out_specs, check_vma=False
    )
```

profile of v0, /device:TPU:32, one launch (start us, length us, event | category | flops | bytes accessed | tf_op | source)
XLA Modules:
  0.0 305.3 jit_solution(1823025273057362841)
XLA Ops:
  6.5 0.0 all-gather.7.cloned.1.call-start
  6.5 0.7 all-gather.7.cloned.1.call-update
  7.3 0.0 all-gather.9.cloned.1.call-start
  7.3 0.7 all-gather.9.cloned.1.call-update
  8.0 24.5 %all-gather.2 = f32[32,224,2]{1,2,0:T(2,128)S(1)} all-gather(f32[1,224,2]{1,2,0:T(2,128)} %bitcast.49), channel_id=1, replica_groups=mesh['row'=8,'col'=32] {'col'}, dimensions={0}, use_global_device_ids=true | all-gather | bytes 59136 | tf_op jit(solution)/shard_map/all_gather | solution.py:17
  32.6 0.1 reshape.144
  32.7 0.7 copy.21
  33.5 0.1 reduce.5
  33.6 0.1 convert_reduce_fusion
  33.7 0.7 broadcast_compare_fusion.1
  34.4 1.0 broadcast_compare_fusion
  35.3 41.2 %all-gather.7.cloned.1.call-done = bf16[384,2,7168]{0,2,1:T(8,128)(2,1)} async-done(((bf16[384,2,224]{0,2,1:T(8,128)(2,1)}), bf16[384,2,7168]{0,2,1:T(8,128)(2,1)}) %all-gather.7.cloned.1.call-update) | async-done | bytes 11010064 | tf_op jit(solution)/shard_map/all_gather | solution.py:16
  76.6 6.3 %fusion = f32[384,2]{0,1:T(2,128)S(1)} fusion(bf16[384,2,7168]{0,2,1:T(8,128)(2,1)} %all-gather.7.cloned.1.call-done), kind=kLoop, calls=%fused_computation.2 | loop fusion | flops 16514304 | bytes 11013120 | tf_op jit(solution)/shard_map/reduce_sum | solution.py:19
  82.9 146.4 %all-gather.9.cloned.1.call-done = bf16[7168,1024]{1,0:T(8,128)(2,1)} async-done(((bf16[896,1024]{1,0:T(8,128)(2,1)}), bf16[7168,1024]{1,0:T(8,128)(2,1)}) %all-gather.9.cloned.1.call-update) | async-done | bytes 14680080 | tf_op jit(solution)/shard_map/all_gather | solution.py:15
  229.3 18.9 %fusion.12 = (f32[384,2]{0,1:T(2,128)S(1)}, f32[384,2,1024]{2,0,1:T(8,128)S(1)}) fusion(bf16[7168,1024]{1,0:T(8,128)(2,1)} %all-gather.9.cloned.1.call-done, bf16[384,2,7168]{0,2,1:T(8,128)(2,1)} %all-gather.7.cloned.1.call-done, f32[2,7168]{1,0:T(2,128)S(1)} %bitcast.42, f32[384,2]{0,1:T(2,128)S(1)} %add_rsqrt_fusion), kind=kOutput, calls=%fused_computation.38 | convolution fusion | flops 11297094656 | bytes 28899328 | tf_op jit(solution)/shard_map/tmd,dv->tmv/dot_general | solution.py:23
  248.2 1.1 exponential_reduce_fusion
  249.3 24.8 %all-gather = f32[96,384,2]{1,2,0:T(2,128)S(1)} all-gather(f32[3,384,2]{1,2,0:T(2,128)S(1)} %pad_maximum_fusion), channel_id=2, replica_groups=mesh['row'=8,'col'=32] {'col'}, dimensions={0}, use_global_device_ids=true | all-gather | bytes 304128 | tf_op jit(solution)/shard_map/all_gather | solution.py:30
  274.1 0.1 bitcast_reduce_fusion
  274.2 0.1 fusion.9
  274.4 0.2 select_reduce_fusion.3
  274.5 23.3 %all-gather.3 = f32[8,3,16]{2,1,0:T(4,128)S(1)} all-gather(f32[1,3,16]{2,1,0:T(4,128)S(1)} %maximum_bitcast_fusion), channel_id=3, replica_groups=mesh['row'=8,'col'=32] {'row'}, dimensions={0}, use_global_device_ids=true | all-gather | bytes 1728 | tf_op jit(solution)/shard_map/all_gather | solution.py:43
  297.9 0.6 copy.25
  (12 shorter events, 0.2 us)
Async XLA Ops:
  6.5 70.0 %all-gather.7.cloned.1.call-start = ((), (), s32[]{:S(2)}) async-start(), calls=%async_computation | async-start | bytes 11354112 | tf_op jit(solution)/shard_map/all_gather | solution.py:16
  7.3 222.0 %all-gather.9.cloned.1.call-start = ((), (), s32[]{:S(2)}) async-start(), calls=%async_computation.1 | async-start | bytes 16515072 | tf_op jit(solution)/shard_map/all_gather | solution.py:15
Sparse Core Ops, SparseCore 0:
  9.9 66.5 all-gather.6
  78.3 150.8 all-gather.8
where the time goes:
time: 306 us; the launch traced here: 305 us
  waiting for transfers between devices  189 us (62%)
  blocking collectives  72.7 us (24%)
  matrix products  18.9 us (6%)
  between operations  13.5 us (4%)
  other arithmetic  9.79 us (3%)
    all_gather x1, waiting for transfers between devices, per_device(): full_unembed = lax.all_gather(unembed, 'row', axis=0, tiled=True)  146 us
    all_gather x1, waiting for transfers between devices, per_device(): full_hidden = lax.all_gather(hidden_in, 'col', axis=2, tiled=True)  41.2 us
    all_gather x1, blocking collectives, per_device(): parts = lax.all_gather(jnp.stack([row_max, exp_total, picked]), 'col')  24.8 us
    all_gather x1, blocking collectives, per_device(): full_gain = lax.all_gather(final_gain, 'col', axis=1, tiled=True)  24.5 us
    all_gather x1, blocking collectives, per_device(): stats = lax.all_gather(jnp.stack([ratio_sums, squares, ratio_max]), 'row')  23.3 us
    dot_general x1, matrix products, per_device(): jnp.einsum('tmd,dv->tmv', features, full_unembed, preferred_element_type=...  18.9 us
    reduce_sum x1, other arithmetic, per_device(): mean_square = jnp.sum(stream * stream, axis=2) / D  6.34 us
  transfers between devices with their start and end apart: 2, of which 2 were waited for; matrix products, arithmetic and copies ran while one was open for 3% of the time, Pallas kernels for 0%

commit v1 on v0

--- a/solution.py
+++ b/solution.py
@@ -12,7 +12,21 @@
     vocab_cols = unembed.shape[1]
     col_index = lax.axis_index("col")
     row_index = lax.axis_index("row")
-    full_unembed = lax.all_gather(unembed, "row", axis=0, tiled=True)
+    ways, here, step = (lax.axis_size("row"), lax.axis_index("row"), unembed.shape[0])
+    lengths_2 = [n * ways if d == 0 else n for d, n in enumerate(unembed.shape)]
+    full = lax.dynamic_update_slice_in_dim(
+        jnp.zeros(lengths_2, unembed.dtype), unembed, here * step, axis=0
+    )
+    going_up = going_down = unembed
+    for far in range(1, ways // 2 + 1):
+        going_up = lax.ppermute(going_up, "row", [(d, (d + 1) % ways) for d in range(ways)])
+        full = lax.dynamic_update_slice_in_dim(full, going_up, (here - far) % ways * step, axis=0)
+        if 2 * far < ways:
+            going_down = lax.ppermute(going_down, "row", [(d, (d - 1) % ways) for d in range(ways)])
+            full = lax.dynamic_update_slice_in_dim(
+                full, going_down, (here + far) % ways * step, axis=0
+            )
+    full_unembed = full
     full_hidden = lax.all_gather(hidden_in, "col", axis=2, tiled=True)
     full_gain = lax.all_gather(final_gain, "col", axis=1, tiled=True)
     stream = full_hidden.astype(jnp.float32)

time: 306 us -> 276 us (0.902)
  waiting for transfers between devices: 189 us -> 119 us
  local copies, waits for them, and re-layouts: 1.43 us -> 31.6 us
  starting transfers between devices: 0.04 us -> 9.45 us
    all_gather x1 -> x0, waiting for transfers between devices: 146 us -> none  [per_device(): full_unembed = lax.all_gather(unembed, 'row', axis=0, tiled=True)]
    ppermute x0 -> x7, waiting for transfers between devices: none -> 118 us  [the longest x4 118 us: per_device(): lax.ppermute(going_up, 'row', [(d, (d + 1) % ways) for d in range(ways)])]
    all_gather x1, waiting for transfers between devices: 41.2 us -> 0.01 us  [per_device(): full_hidden = lax.all_gather(hidden_in, 'col', axis=2, tiled=True)]
    dynamic_update_slice x0 -> x8, local copies, waits for them, and re-layouts: none -> 21.8 us  [the longest x4 11.6 us: per_device(): lax.dynamic_update_slice_in_dim(full, going_up, (here - far) % ways * ste...]
    ppermute x0 -> x7, starting transfers between devices: none -> 9.45 us  [the longest x3 5.53 us: per_device(): lax.ppermute(going_down, 'row', [(d, (d - 1) % ways) for d in range(ways)])]
    broadcast_in_dim x0 -> x1, local copies, waits for them, and re-layouts: none -> 7.1 us  [per_device(): jnp.zeros(lengths_2, unembed.dtype)]
  transfers between devices with their start and end apart: 2 -> 8, of which waited for: 2 -> 3; matrix products, arithmetic and copies ran while one was open for 3% -> 11% of each run, Pallas kernels for 0% -> 0%
where the time goes in v1:
time: 276 us; the launch traced here: 275 us
  waiting for transfers between devices  119 us (43%)
  blocking collectives  74.5 us (27%)
  local copies, waits for them, and re-layouts  31.6 us (11%)
  matrix products  18.9 us (7%)
  between operations  13.5 us (5%)
  starting transfers between devices  9.45 us (3%)
  other arithmetic  8.4 us (3%)
    ppermute x4, waiting for transfers between devices, per_device(): lax.ppermute(going_up, 'row', [(d, (d + 1) % ways) for d in range(ways)])  118 us
    all_gather x1, blocking collectives, per_device(): stats = lax.all_gather(jnp.stack([ratio_sums, squares, ratio_max]), 'row')  25.3 us
    all_gather x1, blocking collectives, per_device(): full_gain = lax.all_gather(final_gain, 'col', axis=1, tiled=True)  24.9 us
    all_gather x1, blocking collectives, per_device(): parts = lax.all_gather(jnp.stack([row_max, exp_total, picked]), 'col')  24.2 us
    dot_general x1, matrix products, per_device(): jnp.einsum('tmd,dv->tmv', features, full_unembed, preferred_element_type=...  18.9 us
    dynamic_update_slice x4, local copies, waits for them, and re-layouts, per_device(): lax.dynamic_update_slice_in_dim(full, going_up, (here - far) % ways * ste...  11.6 us
    dynamic_update_slice x3, local copies, waits for them, and re-layouts, per_device(): lax.dynamic_update_slice_in_dim(full, going_down, (here + far) % ways * s...  8.79 us
    broadcast_in_dim x1, local copies, waits for them, and re-layouts, per_device(): jnp.zeros(lengths_2, unembed.dtype)  7.1 us
  transfers between devices with their start and end apart: 8, of which 3 were waited for; matrix products, arithmetic and copies ran while one was open for 11% of the time, Pallas kernels for 0%

profile of v1, /device:TPU:32, one launch (start us, length us, event | category | flops | bytes accessed | tf_op | source)
XLA Modules:
  0.0 275.2 jit_solution(7017435977189560711)
XLA Ops:
  6.5 0.7 all-gather.6.cloned.1.call-update
  7.3 2.0 collective-permute-start
  9.3 0.1 collective-permute-start.1
  9.4 39.9 %collective-permute-done = bf16[896,1024]{1,0:T(8,128)(2,1)S(1)} collective-permute-done((bf16[896,1024]{1,0:T(8,128)(2,1)}, bf16[896,1024]{1,0:T(8,128)(2,1)S(1)}, u32[]{:S(2)}, u32[]{:S(2)}) %collective-permute-start) | collective-permute-done | bytes 1835040 | tf_op jit(solution)/shard_map/ppermute | solution.py:22
  49.3 1.3 copy-done.1
  50.6 1.9 collective-permute-start.2
  52.5 2.4 collective-permute-start.3
  54.9 39.4 %collective-permute-done.2 = bf16[896,1024]{1,0:T(8,128)(2,1)} collective-permute-done((bf16[896,1024]{1,0:T(8,128)(2,1)S(1)}, bf16[896,1024]{1,0:T(8,128)(2,1)}, u32[]{:S(2)}, u32[]{:S(2)}) %collective-permute-start.2) | collective-permute-done | bytes 1835040 | tf_op jit(solution)/shard_map/ppermute | solution.py:22
  94.4 3.0 %collective-permute-start.5 = (bf16[896,1024]{1,0:T(8,128)(2,1)}, bf16[896,1024]{1,0:T(8,128)(2,1)}, u32[]{:S(2)}, u32[]{:S(2)}) collective-permute-start(bf16[896,1024]{1,0:T(8,128)(2,1)} %collective-permute-done.3), channel_id=1, source_target_pairs={{0,224},{32,0},{64,32},{96,64},{128,96},{160,128},{192,160},{224,1... | collective-permute-start | bytes 5505032 | tf_op jit(solution)/shard_map/ppermute | solution.py:25
  97.4 38.8 %collective-permute-done.4 = bf16[896,1024]{1,0:T(8,128)(2,1)} collective-permute-done((bf16[896,1024]{1,0:T(8,128)(2,1)}, bf16[896,1024]{1,0:T(8,128)(2,1)}, u32[]{:S(2)}, u32[]{:S(2)}) %collective-permute-start.4) | collective-permute-done | bytes 1835040 | tf_op jit(solution)/shard_map/ppermute | solution.py:22
  136.2 24.9 %all-gather.2 = f32[32,224,2]{1,2,0:T(2,128)S(1)} all-gather(f32[1,224,2]{1,2,0:T(2,128)} %bitcast.49), channel_id=1, replica_groups=mesh['row'=8,'col'=32] {'col'}, dimensions={0}, use_global_device_ids=true | all-gather | bytes 59136 | tf_op jit(solution)/shard_map/all_gather | solution.py:31
  161.1 0.1 reshape.144
  161.2 0.7 copy.21
  162.0 0.1 reduce.5
  162.3 7.1 %broadcast_in_dim.71 = bf16[7168,1024]{1,0:T(8,128)(2,1)} broadcast(bf16[]{:T(256)} %constant.71.clone.1), dimensions={} | broadcast | bytes 14680066 | tf_op jit(solution)/shard_map/broadcast_in_dim | solution.py:18
  169.4 1.4 constant_dynamic-update-slice_fusion.7
  170.8 0.3 broadcast_compare_fusion
  171.1 2.9 %constant_dynamic-update-slice_fusion.6 = bf16[7168,1024]{1,0:T(8,128)(2,1)} fusion(bf16[7168,1024]{1,0:T(8,128)(2,1)} %constant_dynamic-update-slice_fusion.7, bf16[896,1024]{1,0:T(8,128)(2,1)} %copy-done.1, s32[]{:T(128)S(6)} %select_n.82), kind=kLoop, calls=%fused_computation.40 | loop fusion | bytes 3670020 | tf_op jit(solution)/shard_map/dynamic_update_slice | solution.py:23
  174.0 2.9 %constant_dynamic-update-slice_fusion.5 = bf16[7168,1024]{1,0:T(8,128)(2,1)} fusion(bf16[7168,1024]{1,0:T(8,128)(2,1)} %constant_dynamic-update-slice_fusion.6, bf16[896,1024]{1,0:T(8,128)(2,1)} %copy-done.2, s32[]{:T(128)S(6)} %select_n.84), kind=kLoop, calls=%fused_computation.39 | loop fusion | bytes 3670020 | tf_op jit(solution)/shard_map/dynamic_update_slice | solution.py:26
  176.8 2.9 %constant_dynamic-update-slice_fusion.4 = bf16[7168,1024]{1,0:T(8,128)(2,1)} fusion(bf16[7168,1024]{1,0:T(8,128)(2,1)} %constant_dynamic-update-slice_fusion.5, bf16[896,1024]{1,0:T(8,128)(2,1)} %collective-permute-done.2, s32[]{:T(128)S(6)} %select_n.86), kind=kLoop, calls=%fused_computation.38 | loop fusion | bytes 3670020 | tf_op jit(solution)/shard_map/dynamic_update_slice | solution.py:23
  179.8 2.9 %constant_dynamic-update-slice_fusion.3 = bf16[7168,1024]{1,0:T(8,128)(2,1)} fusion(bf16[7168,1024]{1,0:T(8,128)(2,1)} %constant_dynamic-update-slice_fusion.4, bf16[896,1024]{1,0:T(8,128)(2,1)} %collective-permute-done.3, s32[]{:T(128)S(6)} %select_n.88), kind=kLoop, calls=%fused_computation.37 | loop fusion | bytes 3670020 | tf_op jit(solution)/shard_map/dynamic_update_slice | solution.py:26
  182.7 2.9 %constant_dynamic-update-slice_fusion.2 = bf16[7168,1024]{1,0:T(8,128)(2,1)} fusion(bf16[7168,1024]{1,0:T(8,128)(2,1)} %constant_dynamic-update-slice_fusion.3, bf16[896,1024]{1,0:T(8,128)(2,1)} %collective-permute-done.4, s32[]{:T(128)S(6)} %select_n.90), kind=kLoop, calls=%fused_computation.36 | loop fusion | bytes 3670020 | tf_op jit(solution)/shard_map/dynamic_update_slice | solution.py:23
  185.6 3.0 %constant_dynamic-update-slice_fusion.1 = bf16[7168,1024]{1,0:T(8,128)(2,1)} fusion(bf16[7168,1024]{1,0:T(8,128)(2,1)} %constant_dynamic-update-slice_fusion.2, bf16[896,1024]{1,0:T(8,128)(2,1)} %collective-permute-done.5, s32[]{:T(128)S(6)} %select_n.92), kind=kLoop, calls=%fused_computation.35 | loop fusion | bytes 3670020 | tf_op jit(solution)/shard_map/dynamic_update_slice | solution.py:26
  188.5 2.9 %constant_dynamic-update-slice_fusion = bf16[7168,1024]{1,0:T(8,128)(2,1)} fusion(bf16[7168,1024]{1,0:T(8,128)(2,1)} %constant_dynamic-update-slice_fusion.1, bf16[896,1024]{1,0:T(8,128)(2,1)} %collective-permute-done.6, s32[]{:T(128)S(6)} %select_n.94), kind=kLoop, calls=%fused_computation.34 | loop fusion | bytes 3670020 | tf_op jit(solution)/shard_map/dynamic_update_slice | solution.py:23
  191.4 6.3 %fusion = f32[384,2]{0,1:T(2,128)S(1)} fusion(bf16[384,2,7168]{0,2,1:T(8,128)(2,1)} %all-gather.6.cloned.1.call-done), kind=kLoop, calls=%fused_computation.2 | loop fusion | flops 16514304 | bytes 11013120 | tf_op jit(solution)/shard_map/reduce_sum | solution.py:33
  197.8 18.9 %fusion.12 = (f32[384,2]{0,1:T(2,128)S(1)}, f32[384,2,1024]{2,0,1:T(8,128)S(1)}) fusion(bf16[7168,1024]{1,0:T(8,128)(2,1)} %constant_dynamic-update-slice_fusion, bf16[384,2,7168]{0,2,1:T(8,128)(2,1)} %all-gather.6.cloned.1.call-done, f32[2,7168]{1,0:T(2,128)S(1)} %bitcast.42, f32[384,2]{0,1:T(2,128)S(1)} %add_rsqrt_fusion), kind=kOutput, calls=%fused_computation.46 | convolution fusion | flops 11297094656 | bytes 28899328 | tf_op jit(solution)/shard_map/tmd,dv->tmv/dot_general | solution.py:37
  216.7 1.1 exponential_reduce_fusion
  217.8 24.2 %all-gather = f32[96,384,2]{1,2,0:T(2,128)S(1)} all-gather(f32[3,384,2]{1,2,0:T(2,128)S(1)} %pad_maximum_fusion), channel_id=2, replica_groups=mesh['row'=8,'col'=32] {'col'}, dimensions={0}, use_global_device_ids=true | all-gather | bytes 304128 | tf_op jit(solution)/shard_map/all_gather | solution.py:44
  242.1 0.1 fusion.9
  242.2 0.2 select_reduce_fusion.3
  242.4 25.3 %all-gather.3 = f32[8,3,16]{2,1,0:T(4,128)S(1)} all-gather(f32[1,3,16]{2,1,0:T(4,128)S(1)} %maximum_bitcast_fusion), channel_id=3, replica_groups=mesh['row'=8,'col'=32] {'row'}, dimensions={0}, use_global_device_ids=true | all-gather | bytes 1728 | tf_op jit(solution)/shard_map/all_gather | solution.py:57
  267.8 0.6 copy.25
  (32 shorter events, 0.4 us)
Async XLA Ops:
  6.5 162.8 %copy-start = (bf16[896,1024]{1,0:T(8,128)(2,1)S(1)}, bf16[896,1024]{1,0:T(8,128)(2,1)}, u32[]{:S(2)}) copy-start(bf16[896,1024]{1,0:T(8,128)(2,1)} %param.8) | copy-start | bytes 5505028
  6.5 164.2 %copy-start.4 = (s32[16]{0:T(128)S(1)}, s32[16]{0:T(128)}, u32[]{:S(2)}) copy-start(s32[16]{0:T(128)} %param.11) | copy-start | bytes 196
  6.5 164.2 %copy-start.3 = (s32[384]{0:T(512)S(1)}, s32[384]{0:T(512)}, u32[]{:S(2)}) copy-start(s32[384]{0:T(512)} %param.10) | copy-start | bytes 4612
  6.5 184.9 %all-gather.6.cloned.1.call-start = ((), (), s32[]{:S(2)}) async-start(), calls=%async_computation | async-start | bytes 11354112 | tf_op jit(solution)/shard_map/all_gather | solution.py:30
  7.3 42.0 %collective-permute-start = (bf16[896,1024]{1,0:T(8,128)(2,1)}, bf16[896,1024]{1,0:T(8,128)(2,1)S(1)}, u32[]{:S(2)}, u32[]{:S(2)}) collective-permute-start(bf16[896,1024]{1,0:T(8,128)(2,1)} %param.8), channel_id=1, source_target_pairs={{0,32},{32,64},{64,96},{96,128},{128,160},{160,192},{192,224},{224... | collective-permute-start | bytes 5505032 | tf_op jit(solution)/shard_map/ppermute | solution.py:22
  9.3 43.2 %collective-permute-start.1 = (bf16[896,1024]{1,0:T(8,128)(2,1)}, bf16[896,1024]{1,0:T(8,128)(2,1)S(1)}, u32[]{:S(2)}, u32[]{:S(2)}) collective-permute-start(bf16[896,1024]{1,0:T(8,128)(2,1)} %param.8), channel_id=1, source_target_pairs={{0,224},{32,0},{64,32},{96,64},{128,96},{160,128},{192,160},{224,1... | collective-permute-start | bytes 5505032 | tf_op jit(solution)/shard_map/ppermute | solution.py:25
  49.3 1.3 copy-start.1
  50.6 43.8 %collective-permute-start.2 = (bf16[896,1024]{1,0:T(8,128)(2,1)S(1)}, bf16[896,1024]{1,0:T(8,128)(2,1)}, u32[]{:S(2)}, u32[]{:S(2)}) collective-permute-start(bf16[896,1024]{1,0:T(8,128)(2,1)S(1)} %collective-permute-done), channel_id=1, source_target_pairs={{0,32},{32,64},{64,96},{96,128},{128,160},{160,192},{192,224},{224... | collective-permute-start | bytes 5505032 | tf_op jit(solution)/shard_map/ppermute | solution.py:22
  52.5 41.8 %copy-start.2 = (bf16[896,1024]{1,0:T(8,128)(2,1)}, bf16[896,1024]{1,0:T(8,128)(2,1)S(1)}, u32[]{:S(2)}) copy-start(bf16[896,1024]{1,0:T(8,128)(2,1)S(1)} %collective-permute-done.1) | copy-start | bytes 5505028
  52.5 41.8 %collective-permute-start.3 = (bf16[896,1024]{1,0:T(8,128)(2,1)S(1)}, bf16[896,1024]{1,0:T(8,128)(2,1)}, u32[]{:S(2)}, u32[]{:S(2)}) collective-permute-start(bf16[896,1024]{1,0:T(8,128)(2,1)S(1)} %collective-permute-done.1), channel_id=1, source_target_pairs={{0,224},{32,0},{64,32},{96,64},{128,96},{160,128},{192,160},{224,1... | collective-permute-start | bytes 5505032 | tf_op jit(solution)/shard_map/ppermute | solution.py:25
  94.3 41.8 %collective-permute-start.4 = (bf16[896,1024]{1,0:T(8,128)(2,1)}, bf16[896,1024]{1,0:T(8,128)(2,1)}, u32[]{:S(2)}, u32[]{:S(2)}) collective-permute-start(bf16[896,1024]{1,0:T(8,128)(2,1)} %collective-permute-done.2), channel_id=1, source_target_pairs={{0,32},{32,64},{64,96},{96,128},{128,160},{160,192},{192,224},{224... | collective-permute-start | bytes 5505032 | tf_op jit(solution)/shard_map/ppermute | solution.py:22
  94.4 91.2 %collective-permute-start.5 = (bf16[896,1024]{1,0:T(8,128)(2,1)}, bf16[896,1024]{1,0:T(8,128)(2,1)}, u32[]{:S(2)}, u32[]{:S(2)}) collective-permute-start(bf16[896,1024]{1,0:T(8,128)(2,1)} %collective-permute-done.3), channel_id=1, source_target_pairs={{0,224},{32,0},{64,32},{96,64},{128,96},{160,128},{192,160},{224,1... | collective-permute-start | bytes 5505032 | tf_op jit(solution)/shard_map/ppermute | solution.py:25
  136.2 52.4 %collective-permute-start.6 = (bf16[896,1024]{1,0:T(8,128)(2,1)}, bf16[896,1024]{1,0:T(8,128)(2,1)}, u32[]{:S(2)}, u32[]{:S(2)}) collective-permute-start(bf16[896,1024]{1,0:T(8,128)(2,1)} %collective-permute-done.4), channel_id=1, source_target_pairs={{0,32},{32,64},{64,96},{96,128},{128,160},{160,192},{192,224},{224... | collective-permute-start | bytes 5505032 | tf_op jit(solution)/shard_map/ppermute | solution.py:22
Sparse Core Ops, SparseCore 0:
  9.9 66.4 all-gather.5
